TPU v7x, 256 devices: a whole 4x4x8 slice. The times are simulated.
256 devices in a mesh: dp: 4 (over x), expert: 64 (over y, z, core).
Axes of the slice: x: 4, y: 4, z: 8, core: 2. Of those that a mesh axis runs over, the one named last changes fastest.
Arguments:
- tokens: bfloat16 [32768, 2048], P(('dp', 'expert')), may hold values from -6 to 6
- expert_ids: int32 [32768, 8], P(('dp', 'expert')), may hold values from 0 to 63, all different within a row; in each aligned block of 128 rows (0 to 127, 128 to 255, ...) at most 24 rows name the same one
- gate_probs: float32 [32768, 8], P(('dp', 'expert')), may hold values from 0.02 to 1
- placement: int32 [64], replicated, may hold values from 0 to 63, each once
- w_gate_up: bfloat16 [64, 2, 768, 2048], P('expert', None, 'dp'), may hold values from -0.125 to 0.125
- w_down: bfloat16 [64, 768, 2048], P('expert', 'dp'), may hold values from -0.21875 to 0.21875
Outputs:
- critic_mix: bfloat16 [32768, 2048], P(('dp', 'expert'))
- placed_gate_up: bfloat16 [64, 2, 768, 2048], P('expert', None, 'dp')
- placed_down: bfloat16 [64, 768, 2048], P('expert', 'dp')
Inputs may be any that keep to these rules, and one draw needn't show every extreme that they name: `expert_ids`: each token names 8 different experts; among the 128 tokens of one device at most 24 name the same expert, and some device reaches 24. `placement`: A permutation of the expert numbers.
All inputs are finite; a program needn't handle non-finite values.
Results may differ from a plain program's by a relative error of at most 0.0058.
Values may be sent and summed in bfloat16 or wider, within the bound.
No kernel may reach another device: no remote copies, remote signals or barrier semaphores. Data moves between devices by JAX's collectives and lax.ppermute only.
A program may use at most 128 MiB of HBM per device.

v0:
```python
import jax
import jax.numpy as jnp
from jax import lax
from jax.sharding import PartitionSpec as P


def per_device(tokens, expert_ids, gate_probs, placement, w_gate_up, w_down):
    tok_dev = tokens.shape[0]
    model_width = tokens.shape[1]
    top_count = expert_ids.shape[1]
    experts = placement.shape[0]
    capacity = min(tok_dev, 3 * tok_dev * top_count // (2 * experts))
    numbers = jnp.arange(experts, dtype=jnp.int32)
    inverse = jnp.sum(
        jnp.where(placement[:, None] == numbers[None, :], numbers[:, None], 0), axis=0
    )
    flat_ids = expert_ids.reshape(-1)
    onehot = (flat_ids[:, None] == numbers[None, :]).astype(jnp.int32)
    before = jnp.cumsum(onehot, axis=0) - onehot
    slot_of = jnp.sum(before * onehot, axis=1)
    down_four = w_down.reshape((1, 1) + w_down.shape[1:])
    pieces = (
        lax.all_to_all(w_gate_up, "expert", split_axis=3, concat_axis=0, tiled=True),
        lax.all_to_all(down_four, "expert", split_axis=3, concat_axis=0, tiled=True),
    )
    reordered = (jnp.take(pieces[0], inverse, axis=0), jnp.take(pieces[1], inverse, axis=0))
    placed = (
        lax.all_to_all(reordered[0], "expert", split_axis=0, concat_axis=3, tiled=True),
        lax.all_to_all(reordered[1], "expert", split_axis=0, concat_axis=3, tiled=True),
    )
    placed_gate_up = placed[0]
    placed_down = placed[1].reshape(w_down.shape)
    gathered = (
        lax.all_gather(placed[0], "dp", axis=2, tiled=True),
        lax.all_gather(placed[1], "dp", axis=2, tiled=True),
    )
    hidden_count = gathered[0].shape[2]
    gate_up_full = gathered[0].reshape(2 * hidden_count, model_width)
    down_full = gathered[1].reshape(hidden_count, model_width)
    flat_index = flat_ids * capacity + slot_of
    spread_rows = jnp.broadcast_to(tokens[:, None, :], (tok_dev, top_count, model_width)).reshape(
        -1, model_width
    )
    buffer = (
        jnp.zeros((experts * capacity, model_width), jnp.bfloat16).at[flat_index].set(spread_rows)
    )
    buffer = buffer.reshape(experts, capacity, model_width)
    received = lax.all_to_all(buffer, "expert", split_axis=0, concat_axis=0, tiled=True)
    row_block = received.reshape(-1, model_width)
    projected = lax.dot_general(
        row_block, gate_up_full, (((1,), (1,)), ((), ())), preferred_element_type=jnp.float32
    )
    gate_part = projected[:, :hidden_count]
    up_part = projected[:, hidden_count:]
    hidden = (jax.nn.silu(gate_part) * up_part).astype(jnp.bfloat16)
    result = jnp.dot(hidden, down_full, preferred_element_type=jnp.float32).astype(jnp.bfloat16)
    result = result.reshape(received.shape)
    returned = lax.all_to_all(result, "expert", split_axis=0, concat_axis=0, tiled=True)
    flat_out = returned.reshape(experts * capacity, model_width)
    picked = flat_out[flat_index].reshape(tok_dev, top_count, model_width)
    gates = gate_probs / jnp.sum(gate_probs, axis=1, keepdims=True)
    mixed_rows = jnp.einsum(
        "tk,tkd->td",
        gates,
        picked,
        preferred_element_type=jnp.float32,
        precision=lax.Precision.HIGHEST,
    )
    return (mixed_rows.astype(jnp.bfloat16), placed_gate_up, placed_down)


def solution(mesh):
    in_specs = (
        P(("dp", "expert"), None),
        P(("dp", "expert"), None),
        P(("dp", "expert"), None),
        P(),
        P("expert", None, "dp", None),
        P("expert", "dp", None),
    )
    out_specs = (P(("dp", "expert"), None), P("expert", None, "dp", None), P("expert", "dp", None))
    return jax.shard_map(
        per_device, mesh=mesh, in_specs=in_specs, out_specs=out_specs, check_vma=False
    )
```

profile of v0, /device:TPU:1, one launch (start us, length us, event | category | flops | bytes accessed | tf_op | source)
XLA Modules:
  0.0 561.2 jit_solution(7574284037175607885)
XLA Ops:
  7.2 4.6 copy.75
  12.3 12.6 %reduce = bf16[2048,192]{1,0:T(8,128)(2,1)} reduce(bf16[2048,1,1,192]{3,2,1,0:T(2,128)(2,1)S(1)} %bitcast.83, bf16[]{:T(256)} %broadcast.106), dimensions={1,2}, to_apply=%bitcast.70.reduce_sub_computation | reduce | bytes 1572866
  24.9 3.7 reshape.162
  28.6 13.2 %all-to-all-start.3 = ((bf16[64,2,3072]{2,1,0:T(2,128)(2,1)}), bf16[64,2,3072]{2,1,0:T(2,128)(2,1)S(1)}, u32[]{:S(2)}, u32[]{:S(2)}) async-start(bf16[64,2,3072]{2,1,0:T(2,128)(2,1)} %reshape.162), calls=%async_computation.3 | async-start | bytes 1572864 | tf_op jit(solution)/shard_map/all_to_all | solution.py:24
  41.8 3.8 copy.69
  45.5 19.2 %all-to-all-done.3 = bf16[64,2,3072]{2,1,0:T(2,128)(2,1)S(1)} async-done(((bf16[64,2,3072]{2,1,0:T(2,128)(2,1)}), bf16[64,2,3072]{2,1,0:T(2,128)(2,1)S(1)}, u32[]{:S(2)}, u32[]{:S(2)}) %all-to-all-start.3) | async-done | bytes 786464 | tf_op jit(solution)/shard_map/all_to_all | solution.py:24
  64.7 6.4 %all-to-all-start.1 = ((bf16[1,2,192,2048]{2,1,0,3:T(2,128)(2,1)}), bf16[1,2,192,2048]{2,1,0,3:T(2,128)(2,1)}, u32[]{:S(2)}, u32[]{:S(2)}) async-start(bf16[1,2,192,2048]{2,1,0,3:T(2,128)(2,1)} %copy.69), calls=%async_computation.1 | async-start | bytes 4194304 | tf_op jit(solution)/shard_map/all_to_all | solution.py:23
  71.2 3.7 reshape.163
  78.5 43.8 %all-to-all-done.1 = bf16[1,2,192,2048]{2,1,0,3:T(2,128)(2,1)} async-done(((bf16[1,2,192,2048]{2,1,0,3:T(2,128)(2,1)}), bf16[1,2,192,2048]{2,1,0,3:T(2,128)(2,1)}, u32[]{:S(2)}, u32[]{:S(2)}) %all-to-all-start.1) | async-done | bytes 1572896 | tf_op jit(solution)/shard_map/all_to_all | solution.py:23
  122.3 6.0 %all-to-all-start.4 = ((bf16[64,1,192,32]{2,3,1,0:T(8,128)(2,1)}), bf16[64,1,192,32]{2,3,1,0:T(8,128)(2,1)}, u32[]{:S(2)}, u32[]{:S(2)}) async-start(bf16[64,1,192,32]{2,3,1,0:T(8,128)(2,1)} %fusion.10), calls=%async_computation.4 | async-start | bytes 2097152 | tf_op jit(solution)/shard_map/all_to_all | solution.py:29
  128.3 3.4 copy.89
  131.7 2.3 gather_fusion
  135.6 21.2 %all-to-all-done.4 = bf16[64,1,192,32]{2,3,1,0:T(8,128)(2,1)} async-done(((bf16[64,1,192,32]{2,3,1,0:T(8,128)(2,1)}), bf16[64,1,192,32]{2,3,1,0:T(8,128)(2,1)}, u32[]{:S(2)}, u32[]{:S(2)}) %all-to-all-start.4) | async-done | bytes 786464 | tf_op jit(solution)/shard_map/all_to_all | solution.py:29
  156.8 6.2 %all-to-all-start.2 = ((bf16[64,2,192,32]{2,3,1,0:T(8,128)(2,1)}), bf16[64,2,192,32]{2,3,1,0:T(8,128)(2,1)S(1)}, u32[]{:S(2)}, u32[]{:S(2)}) async-start(bf16[64,2,192,32]{2,3,1,0:T(8,128)(2,1)} %broadcast_select_fusion), calls=%async_computation.2 | async-start | bytes 4194304 | tf_op jit(solution)/shard_map/all_to_all | solution.py:28
  163.3 18.0 %reduce-window.6 = s32[64,8,128]{2,1,0:T(8,128)S(1)} reduce-window(s32[64,8,128]{2,1,0:T(8,128)S(1)} %fusion.14, s32[]{:T(128)} %constant.32.clone.1), window={size=1x1x128 pad=0_0x0_0x127_0}, to_apply=%region_1.2 | reduce-window | flops 8323072 | bytes 524292 | tf_op jit(solution)/shard_map/reduce-window
  182.2 10.2 %scatter_custom_fusion = bf16[1536,2048]{1,0:T(8,128)(2,1)} fusion(s32[1024]{0:T(1024)S(1)} %bitcast.92, bf16[]{:T(256)} %constant.24.clone.1, bf16[128,2048]{1,0:T(8,128)(2,1)S(1)} %copy-done), kind=kCustom, calls=%fused_computation.9 | custom fusion | bytes 6815746 | tf_op jit(solution)/shard_map/scatter | solution.py:45
  192.4 21.8 %all-to-all-done.2 = bf16[64,2,192,32]{2,3,1,0:T(8,128)(2,1)S(1)} async-done(((bf16[64,2,192,32]{2,3,1,0:T(8,128)(2,1)}), bf16[64,2,192,32]{2,3,1,0:T(8,128)(2,1)S(1)}, u32[]{:S(2)}, u32[]{:S(2)}) %all-to-all-start.2) | async-done | bytes 1572896 | tf_op jit(solution)/shard_map/all_to_all | solution.py:28
  214.2 6.0 %all-to-all-start = ((bf16[64,24,2048]{2,1,0:T(8,128)(2,1)}), bf16[64,24,2048]{2,1,0:T(8,128)(2,1)}, u32[]{:S(2)}, u32[]{:S(2)}) async-start(bf16[64,24,2048]{2,1,0:T(8,128)(2,1)} %bitcast.78), calls=%async_computation | async-start | bytes 12582912 | tf_op jit(solution)/shard_map/all_to_all | solution.py:48
  220.3 1.8 copy.72
  222.1 3.3 copy.73
  225.7 2.2 copy.77
  227.9 66.8 %all-gather.3.cloned.1.call-done = bf16[1,2,768,2048]{3,1,0,2:T(2,128)(2,1)} async-done(((bf16[1,2,192,2048]{3,1,0,2:T(2,128)(2,1)}), bf16[1,2,768,2048]{3,1,0,2:T(2,128)(2,1)}) %all-gather.3.cloned.1.call-update) | async-done | bytes 6291472 | tf_op jit(solution)/shard_map/all_gather | solution.py:34
  294.7 8.3 %copy.74 = bf16[1,2,768,2048]{3,2,1,0:T(8,128)(2,1)} copy(bf16[1,2,768,2048]{3,1,0,2:T(2,128)(2,1)} %all-gather.3.cloned.1.call-done) | data formatting | bytes 12582912 | tf_op jit(solution)/shard_map/all_gather | solution.py:34
  303.0 58.0 %all-to-all-done = bf16[64,24,2048]{2,1,0:T(8,128)(2,1)} async-done(((bf16[64,24,2048]{2,1,0:T(8,128)(2,1)}), bf16[64,24,2048]{2,1,0:T(8,128)(2,1)}, u32[]{:S(2)}, u32[]{:S(2)}) %all-to-all-start) | async-done | bytes 6291488 | tf_op jit(solution)/shard_map/all_to_all | solution.py:48
  361.0 15.7 %fusion.17 = f32[1536,1536]{1,0:T(8,128)} fusion(bf16[1536,2048]{1,0:T(8,128)(2,1)} %bitcast.7, bf16[1536,2048]{1,0:T(8,128)(2,1)} %bitcast.86), kind=kOutput, calls=%fused_computation.40 | convolution fusion | flops 9663676416 | bytes 22020096 | tf_op jit(solution)/shard_map/dot_general | solution.py:50
  376.8 11.4 %convolution_convert_fusion = bf16[1536,2048]{1,0:T(8,128)(2,1)} fusion(bf16[1,1,768,2048]{3,2,1,0:T(8,128)(2,1)} %all-gather.5.cloned.1.call-done, f32[1536,1536]{1,0:T(8,128)} %fusion.17), kind=kOutput, calls=%fused_computation.4 | convolution fusion | flops 4842061824 | bytes 18874368 | tf_op jit(solution)/shard_map/dot_general | solution.py:56
  388.1 6.1 %all-to-all-start.5 = ((bf16[64,24,2048]{2,1,0:T(8,128)(2,1)}), bf16[64,24,2048]{2,1,0:T(8,128)(2,1)}, u32[]{:S(2)}, u32[]{:S(2)}) async-start(bf16[64,24,2048]{2,1,0:T(8,128)(2,1)} %bitcast.85), calls=%async_computation.5 | async-start | bytes 12582912 | tf_op jit(solution)/shard_map/all_to_all | solution.py:58
  394.4 2.2 copy.79
  396.6 2.2 copy.78
  398.8 136.3 %all-to-all-done.5 = bf16[64,24,2048]{2,1,0:T(8,128)(2,1)} async-done(((bf16[64,24,2048]{2,1,0:T(8,128)(2,1)}), bf16[64,24,2048]{2,1,0:T(8,128)(2,1)}, u32[]{:S(2)}, u32[]{:S(2)}) %all-to-all-start.5) | async-done | bytes 6291488 | tf_op jit(solution)/shard_map/all_to_all | solution.py:58
  535.1 12.4 %gather_fusion.2 = bf16[1024,2048]{1,0:T(8,128)(2,1)} fusion(bf16[1536,2048]{1,0:T(8,128)(2,1)} %bitcast.27, s32[1024]{0:T(1024)S(1)} %broadcast_clamp_fusion), kind=kCustom, calls=%fused_computation.2 | custom fusion | bytes 8392704 | tf_op jit(solution)/shard_map/gather | solution.py:60
  547.5 5.7 %fusion.1 = bf16[128,1,2048]{2,1,0:T(2,128)(2,1)S(1)} fusion(f32[128,8,1]{1,2,0:T(1,128)S(1)} %copy.80, bf16[1024,2048]{1,0:T(8,128)(2,1)} %gather_fusion.2), kind=kOutput, calls=%fused_computation.7 | convolution fusion | flops 25165824 | bytes 4722688 | tf_op jit(solution)/shard_map/tk,tkd->td/dot_general | solution.py:62
  (48 shorter events, 8.5 us)
Async XLA Ops:
  7.2 175.0 %copy-start = (bf16[128,2048]{1,0:T(8,128)(2,1)S(1)}, bf16[128,2048]{1,0:T(8,128)(2,1)}, u32[]{:S(2)}) copy-start(bf16[128,2048]{1,0:T(8,128)(2,1)} %param.6) | copy-start | bytes 1572868
  24.9 16.8 %copy-start.3 = (bf16[1,2,192,2048]{3,2,1,0:T(8,128)(2,1)S(1)}, bf16[1,2,192,2048]{3,2,1,0:T(8,128)(2,1)}, u32[]{:S(2)}) copy-start(bf16[1,2,192,2048]{3,2,1,0:T(8,128)(2,1)} %param.10) | copy-start | bytes 4718596
  28.6 36.1 %all-to-all-start.3 = ((bf16[64,2,3072]{2,1,0:T(2,128)(2,1)}), bf16[64,2,3072]{2,1,0:T(2,128)(2,1)S(1)}, u32[]{:S(2)}, u32[]{:S(2)}) async-start(bf16[64,2,3072]{2,1,0:T(2,128)(2,1)} %reshape.162), calls=%async_computation.3 | async-start | bytes 1572864 | tf_op jit(solution)/shard_map/all_to_all | solution.py:24
  41.7 29.4 %copy-start.6 = (s32[64]{0:T(128)S(1)}, s32[64]{0:T(128)}, u32[]{:S(2)}) copy-start(s32[64]{0:T(128)} %param.9) | copy-start | bytes 772
  64.7 57.6 %all-to-all-start.1 = ((bf16[1,2,192,2048]{2,1,0,3:T(2,128)(2,1)}), bf16[1,2,192,2048]{2,1,0,3:T(2,128)(2,1)}, u32[]{:S(2)}, u32[]{:S(2)}) async-start(bf16[1,2,192,2048]{2,1,0,3:T(2,128)(2,1)} %copy.69), calls=%async_computation.1 | async-start | bytes 4194304 | tf_op jit(solution)/shard_map/all_to_all | solution.py:23
  122.3 34.5 %all-to-all-start.4 = ((bf16[64,1,192,32]{2,3,1,0:T(8,128)(2,1)}), bf16[64,1,192,32]{2,3,1,0:T(8,128)(2,1)}, u32[]{:S(2)}, u32[]{:S(2)}) async-start(bf16[64,1,192,32]{2,3,1,0:T(8,128)(2,1)} %fusion.10), calls=%async_computation.4 | async-start | bytes 2097152 | tf_op jit(solution)/shard_map/all_to_all | solution.py:29
  133.9 29.0 %copy-start.4 = (s32[128,8]{0,1:T(8,128)S(1)}, s32[128,8]{0,1:T(8,128)}, u32[]{:S(2)}) copy-start(s32[128,8]{0,1:T(8,128)} %param.7) | copy-start | bytes 12292
  156.8 57.4 %all-to-all-start.2 = ((bf16[64,2,192,32]{2,3,1,0:T(8,128)(2,1)}), bf16[64,2,192,32]{2,3,1,0:T(8,128)(2,1)S(1)}, u32[]{:S(2)}, u32[]{:S(2)}) async-start(bf16[64,2,192,32]{2,3,1,0:T(8,128)(2,1)} %broadcast_select_fusion), calls=%async_computation.2 | async-start | bytes 4194304 | tf_op jit(solution)/shard_map/all_to_all | solution.py:28
  214.2 6.0 %copy-start.2 = (bf16[64,2,192,32]{2,3,1,0:T(8,128)(2,1)}, bf16[64,2,192,32]{2,3,1,0:T(8,128)(2,1)S(1)}, u32[]{:S(2)}) copy-start(bf16[64,2,192,32]{2,3,1,0:T(8,128)(2,1)S(1)} %all-to-all-done.2) | copy-start | bytes 4718596
  214.2 146.8 %all-to-all-start = ((bf16[64,24,2048]{2,1,0:T(8,128)(2,1)}), bf16[64,24,2048]{2,1,0:T(8,128)(2,1)}, u32[]{:S(2)}, u32[]{:S(2)}) async-start(bf16[64,24,2048]{2,1,0:T(8,128)(2,1)} %bitcast.78), calls=%async_computation | async-start | bytes 12582912 | tf_op jit(solution)/shard_map/all_to_all | solution.py:48
  220.2 74.5 %all-gather.3.cloned.1.call-start = ((), (), s32[]{:S(2)}) async-start(), calls=%async_computation.6 | async-start | bytes 7864320 | tf_op jit(solution)/shard_map/all_gather | solution.py:34
  225.4 151.3 %all-gather.5.cloned.1.call-start = ((), (), s32[]{:S(2)}) async-start(), calls=%async_computation.7 | async-start | bytes 3932160 | tf_op jit(solution)/shard_map/all_gather | solution.py:35
  388.1 6.1 %copy-start.5 = (f32[128,8]{0,1:T(8,128)S(1)}, f32[128,8]{0,1:T(8,128)}, u32[]{:S(2)}) copy-start(f32[128,8]{0,1:T(8,128)} %param.8) | copy-start | bytes 12292
  388.1 146.9 %all-to-all-start.5 = ((bf16[64,24,2048]{2,1,0:T(8,128)(2,1)}), bf16[64,24,2048]{2,1,0:T(8,128)(2,1)}, u32[]{:S(2)}, u32[]{:S(2)}) async-start(bf16[64,24,2048]{2,1,0:T(8,128)(2,1)} %bitcast.85), calls=%async_computation.5 | async-start | bytes 12582912 | tf_op jit(solution)/shard_map/all_to_all | solution.py:58
  535.1 19.3 %copy-start.1 = (bf16[128,2048]{1,0:T(8,128)(2,1)S(1)}, bf16[128,2048]{1,0:T(8,128)(2,1)}, u32[]{:S(2)}) copy-start(bf16[128,2048]{1,0:T(8,128)(2,1)} %param.6) | copy-start | bytes 1572868
Sparse Core Ops, SparseCore 0:
  225.5 69.1 all-gather.2
  297.1 42.7 all-gather.4
where the time goes:
time: 562 us; the launch traced here: 561 us
  waiting for transfers between devices  367 us (65%)
  local copies, waits for them, and re-layouts  69.1 us (12%)
  starting transfers between devices  44.1 us (8%)
  other arithmetic  33.8 us (6%)
  matrix products  32.8 us (6%)
  between operations  14.3 us (3%)
    all_to_all x1, waiting for transfers between devices, per_device(): lax.all_to_all(result, 'expert', split_axis=0, concat_axis=0, tiled=True)  136 us
    all_gather x1, waiting for transfers between devices, per_device(): lax.all_gather(placed[0], 'dp', axis=2, tiled=True)  66.8 us
    all_to_all x1, waiting for transfers between devices, per_device(): lax.all_to_all(buffer, 'expert', split_axis=0, concat_axis=0, tiled=True)  58 us
    all_to_all x1, waiting for transfers between devices, per_device(): lax.all_to_all(w_gate_up, 'expert', split_axis=3, concat_axis=0, tiled=True)  43.8 us
    all_to_all x1, waiting for transfers between devices, per_device(): lax.all_to_all(reordered[0], 'expert', split_axis=0, concat_axis=3, tiled...  21.8 us
    all_to_all x1, waiting for transfers between devices, per_device(): lax.all_to_all(reordered[1], 'expert', split_axis=0, concat_axis=3, tiled...  21.2 us
    all_to_all x1, waiting for transfers between devices, per_device(): lax.all_to_all(down_four, 'expert', split_axis=3, concat_axis=0, tiled=True)  19.2 us
    another operation x3, other arithmetic  18.2 us
  transfers between devices with their start and end apart: 8, of which 7 were waited for; matrix products, arithmetic and copies ran while one was open for 15% of the time, Pallas kernels for 0%

commit v1 on v0

--- a/solution.py
+++ b/solution.py
@@ -2,6 +2,18 @@
 import jax.numpy as jnp
 from jax import lax
 from jax.sharding import PartitionSpec as P
+
+
+def order_forms(z_in, dim_at):
+    total_devices = lax.axis_size("dp")
+    long_array = lax.all_to_all(
+        jnp.tile(z_in, list(map(lambda t: total_devices if t == dim_at else 1, range(z_in.ndim)))),
+        axis_name="dp",
+        split_axis=dim_at,
+        concat_axis=dim_at,
+        tiled=True,
+    )
+    return long_array
 
 
 def per_device(tokens, expert_ids, gate_probs, placement, w_gate_up, w_down):
@@ -30,10 +42,7 @@
     )
     placed_gate_up = placed[0]
     placed_down = placed[1].reshape(w_down.shape)
-    gathered = (
-        lax.all_gather(placed[0], "dp", axis=2, tiled=True),
-        lax.all_gather(placed[1], "dp", axis=2, tiled=True),
-    )
+    gathered = (order_forms(placed[0], 2), lax.all_gather(placed[1], "dp", axis=2, tiled=True))
     hidden_count = gathered[0].shape[2]
     gate_up_full = gathered[0].reshape(2 * hidden_count, model_width)
     down_full = gathered[1].reshape(hidden_count, model_width)

time: 562 us -> 630 us (1.12)
  waiting for transfers between devices: 367 us -> 421 us
    all_to_all x1, waiting for transfers between devices: 58 us -> 130 us  [per_device(): lax.all_to_all(buffer, 'expert', split_axis=0, concat_axis=0, tiled=True)]
    all_gather x1 -> x0, waiting for transfers between devices: 66.8 us -> none  [per_device(): lax.all_gather(placed[0], 'dp', axis=2, tiled=True)]
    all_to_all x0 -> x1, waiting for transfers between devices: none -> 41.9 us  [order_forms(): lax.all_to_all(jnp.tile(z_in, list(map(lambda t: total_devices if t == di...]
    all_to_all x1, waiting for transfers between devices: 21.8 us -> 43.9 us  [per_device(): lax.all_to_all(reordered[0], 'expert', split_axis=0, concat_axis=3, tiled...]
    all_to_all x1, waiting for transfers between devices: 43.8 us -> 29.8 us  [per_device(): lax.all_to_all(w_gate_up, 'expert', split_axis=3, concat_axis=0, tiled=True)]
    another operation x2 -> x4, local copies, waits for them, and re-layouts: 0.09 us -> 9.33 us  [the longest x2 9.25 us: order_forms(): jnp.tile(z_in, list(map(lambda t: total_devices if t == dim_at else 1, ra...]
    all_to_all x0 -> x1, local copies, waits for them, and re-layouts: none -> 8.33 us  [order_forms(): lax.all_to_all(jnp.tile(z_in, list(map(lambda t: total_devices if t == di...]
    all_gather x1 -> x0, local copies, waits for them, and re-layouts: 8.29 us -> none  [per_device(): lax.all_gather(placed[0], 'dp', axis=2, tiled=True)]
  transfers between devices with their start and end apart: 8 -> 8, of which waited for: 7 -> 7; matrix products, arithmetic and copies ran while one was open for 15% -> 16% of each run, Pallas kernels for 0% -> 0%
where the time goes in v1:
time: 630 us; the launch traced here: 629 us
  waiting for transfers between devices  421 us (67%)
  local copies, waits for them, and re-layouts  74.9 us (12%)
  starting transfers between devices  49.9 us (8%)
  other arithmetic  36.4 us (6%)
  matrix products  32.7 us (5%)
  between operations  14.3 us (2%)
    all_to_all x1, waiting for transfers between devices, per_device(): lax.all_to_all(result, 'expert', split_axis=0, concat_axis=0, tiled=True)  136 us
    all_to_all x1, waiting for transfers between devices, per_device(): lax.all_to_all(buffer, 'expert', split_axis=0, concat_axis=0, tiled=True)  130 us
    all_to_all x1, waiting for transfers between devices, per_device(): lax.all_to_all(reordered[0], 'expert', split_axis=0, concat_axis=3, tiled...  43.9 us
    all_to_all x1, waiting for transfers between devices, order_forms(): lax.all_to_all(jnp.tile(z_in, list(map(lambda t: total_devices if t == di...  41.9 us
    all_to_all x1, waiting for transfers between devices, per_device(): lax.all_to_all(w_gate_up, 'expert', split_axis=3, concat_axis=0, tiled=True)  29.8 us
    all_to_all x1, waiting for transfers between devices, per_device(): lax.all_to_all(reordered[1], 'expert', split_axis=0, concat_axis=3, tiled...  23.3 us
    unnamed x22, local copies, waits for them, and re-layouts  20.3 us
    another operation x3, other arithmetic  18.2 us
  transfers between devices with their start and end apart: 8, of which 7 were waited for; matrix products, arithmetic and copies ran while one was open for 16% of the time, Pallas kernels for 0%

profile of v1, /device:TPU:1, one launch (start us, length us, event | category | flops | bytes accessed | tf_op | source)
XLA Modules:
  0.0 628.8 jit_solution(14701997997527123295)
XLA Ops:
  7.2 6.1 copy.60
  13.3 13.2 %all-to-all-start.1 = ((bf16[1,2,192,2048]{2,1,0,3:T(2,128)(2,1)}), bf16[1,2,192,2048]{2,1,0,3:T(2,128)(2,1)S(1)}, u32[]{:S(2)}, u32[]{:S(2)}) async-start(bf16[1,2,192,2048]{2,1,0,3:T(2,128)(2,1)} %copy.60), calls=%async_computation.1 | async-start | bytes 4194304 | tf_op jit(solution)/shard_map/all_to_all | solution.py:35
  26.5 3.7 copy.66
  30.8 13.6 %reduce = bf16[2048,192]{1,0:T(8,128)(2,1)} reduce(bf16[2048,1,1,192]{3,2,1,0:T(2,128)(2,1)} %bitcast.86, bf16[]{:T(256)} %broadcast.109), dimensions={1,2}, to_apply=%bitcast.72.reduce_sub_computation | reduce | bytes 1572866
  44.4 3.5 reshape.169
  48.0 29.8 %all-to-all-done.1 = bf16[1,2,192,2048]{2,1,0,3:T(2,128)(2,1)S(1)} async-done(((bf16[1,2,192,2048]{2,1,0,3:T(2,128)(2,1)}), bf16[1,2,192,2048]{2,1,0,3:T(2,128)(2,1)S(1)}, u32[]{:S(2)}, u32[]{:S(2)}) %all-to-all-start.1) | async-done | bytes 1572896 | tf_op jit(solution)/shard_map/all_to_all | solution.py:35
  77.8 5.8 all-to-all-start.4
  87.8 3.2 broadcast_select_fusion
  91.0 15.6 %all-to-all-done.4 = bf16[64,2,3072]{2,1,0:T(2,128)(2,1)S(1)} async-done(((bf16[64,2,3072]{2,1,0:T(2,128)(2,1)}), bf16[64,2,3072]{2,1,0:T(2,128)(2,1)S(1)}, u32[]{:S(2)}, u32[]{:S(2)}) %all-to-all-start.4) | async-done | bytes 786464 | tf_op jit(solution)/shard_map/all_to_all | solution.py:36
  106.6 6.4 %all-to-all-start.2 = ((bf16[64,2,192,32]{2,3,1,0:T(8,128)(2,1)}), bf16[64,2,192,32]{2,3,1,0:T(8,128)(2,1)}, u32[]{:S(2)}, u32[]{:S(2)}) async-start(bf16[64,2,192,32]{2,3,1,0:T(8,128)(2,1)} %broadcast_select_fusion), calls=%async_computation.2 | async-start | bytes 4194304 | tf_op jit(solution)/shard_map/all_to_all | solution.py:40
  113.0 3.8 reshape.170
  120.3 43.9 %all-to-all-done.2 = bf16[64,2,192,32]{2,3,1,0:T(8,128)(2,1)} async-done(((bf16[64,2,192,32]{2,3,1,0:T(8,128)(2,1)}), bf16[64,2,192,32]{2,3,1,0:T(8,128)(2,1)}, u32[]{:S(2)}, u32[]{:S(2)}) %all-to-all-start.2) | async-done | bytes 1572896 | tf_op jit(solution)/shard_map/all_to_all | solution.py:40
  164.1 6.0 all-to-all-start.5
  171.9 3.3 copy.64
  175.3 23.3 %all-to-all-done.5 = bf16[64,1,192,32]{2,3,1,0:T(8,128)(2,1)} async-done(((bf16[64,1,192,32]{2,3,1,0:T(8,128)(2,1)}), bf16[64,1,192,32]{2,3,1,0:T(8,128)(2,1)}, u32[]{:S(2)}, u32[]{:S(2)}) %all-to-all-start.5) | async-done | bytes 786464 | tf_op jit(solution)/shard_map/all_to_all | solution.py:41
  198.6 5.9 tile.12
  204.5 5.5 all-to-all-start.3
  210.4 18.0 %reduce-window.6 = s32[64,8,128]{2,1,0:T(8,128)S(1)} reduce-window(s32[64,8,128]{2,1,0:T(8,128)S(1)} %fusion.14, s32[]{:T(128)} %constant.32.clone.1), window={size=1x1x128 pad=0_0x0_0x127_0}, to_apply=%region_1.2 | reduce-window | flops 8323072 | bytes 524292 | tf_op jit(solution)/shard_map/reduce-window
  229.2 10.2 %scatter_custom_fusion = bf16[1536,2048]{1,0:T(8,128)(2,1)} fusion(s32[1024]{0:T(1024)S(1)} %bitcast.95, bf16[]{:T(256)} %constant.24.clone.1, bf16[128,2048]{1,0:T(8,128)(2,1)S(1)} %copy-done), kind=kCustom, calls=%fused_computation.9 | custom fusion | bytes 6815746 | tf_op jit(solution)/shard_map/scatter | solution.py:54
  239.4 41.9 %all-to-all-done.3 = bf16[1,2,768,2048]{3,1,0,2:T(2,128)(2,1)} async-done(((bf16[1,2,768,2048]{3,1,0,2:T(2,128)(2,1)}), bf16[1,2,768,2048]{3,1,0,2:T(2,128)(2,1)}, u32[]{:S(2)}, u32[]{:S(2)}) %all-to-all-start.3) | async-done | bytes 6291488 | tf_op jit(solution)/shard_map/all_to_all | solution.py:9
  281.3 6.6 %all-to-all-start = ((bf16[64,24,2048]{2,1,0:T(8,128)(2,1)}), bf16[64,24,2048]{2,1,0:T(8,128)(2,1)}, u32[]{:S(2)}, u32[]{:S(2)}) async-start(bf16[64,24,2048]{2,1,0:T(8,128)(2,1)} %bitcast.80), calls=%async_computation | async-start | bytes 12582912 | tf_op jit(solution)/shard_map/all_to_all | solution.py:57
  288.2 2.2 copy.68
  290.4 8.3 %copy.65 = bf16[1,2,768,2048]{3,2,1,0:T(8,128)(2,1)} copy(bf16[1,2,768,2048]{3,1,0,2:T(2,128)(2,1)} %all-to-all-done.3) | data formatting | bytes 12582912 | tf_op jit(solution)/shard_map/all_to_all | solution.py:9
  298.8 130.0 %all-to-all-done = bf16[64,24,2048]{2,1,0:T(8,128)(2,1)} async-done(((bf16[64,24,2048]{2,1,0:T(8,128)(2,1)}), bf16[64,24,2048]{2,1,0:T(8,128)(2,1)}, u32[]{:S(2)}, u32[]{:S(2)}) %all-to-all-start) | async-done | bytes 6291488 | tf_op jit(solution)/shard_map/all_to_all | solution.py:57
  428.8 15.6 %fusion.17 = f32[1536,1536]{1,0:T(8,128)} fusion(bf16[1536,2048]{1,0:T(8,128)(2,1)} %bitcast.7, bf16[1536,2048]{1,0:T(8,128)(2,1)} %bitcast.89), kind=kOutput, calls=%fused_computation.40 | convolution fusion | flops 9663676416 | bytes 22020096 | tf_op jit(solution)/shard_map/dot_general | solution.py:59
  444.4 11.4 %convolution_convert_fusion = bf16[1536,2048]{1,0:T(8,128)(2,1)} fusion(bf16[1,1,768,2048]{3,2,1,0:T(8,128)(2,1)} %all-gather.2.cloned.1.call-done, f32[1536,1536]{1,0:T(8,128)} %fusion.17), kind=kOutput, calls=%fused_computation.4 | convolution fusion | flops 4842061824 | bytes 18874368 | tf_op jit(solution)/shard_map/dot_general | solution.py:65
  455.8 6.1 all-to-all-start.6
  462.0 2.2 copy.71
  464.2 2.2 copy.70
  466.4 136.3 %all-to-all-done.6 = bf16[64,24,2048]{2,1,0:T(8,128)(2,1)} async-done(((bf16[64,24,2048]{2,1,0:T(8,128)(2,1)}), bf16[64,24,2048]{2,1,0:T(8,128)(2,1)}, u32[]{:S(2)}, u32[]{:S(2)}) %all-to-all-start.6) | async-done | bytes 6291488 | tf_op jit(solution)/shard_map/all_to_all | solution.py:67
  602.7 12.5 %gather_fusion.2 = bf16[1024,2048]{1,0:T(8,128)(2,1)} fusion(bf16[1536,2048]{1,0:T(8,128)(2,1)} %bitcast.28, s32[1024]{0:T(1024)S(1)} %broadcast_clamp_fusion), kind=kCustom, calls=%fused_computation.2 | custom fusion | bytes 8392704 | tf_op jit(solution)/shard_map/gather | solution.py:69
  615.2 5.7 fusion.1
  (48 shorter events, 12.7 us)
Async XLA Ops:
  7.2 222.1 %copy-start = (bf16[128,2048]{1,0:T(8,128)(2,1)S(1)}, bf16[128,2048]{1,0:T(8,128)(2,1)}, u32[]{:S(2)}) copy-start(bf16[128,2048]{1,0:T(8,128)(2,1)} %param.6) | copy-start | bytes 1572868
  7.2 19.3 %copy-start.3 = (bf16[1,192,2048]{2,1,0:T(8,128)(2,1)S(1)}, bf16[1,192,2048]{2,1,0:T(8,128)(2,1)}, u32[]{:S(2)}) copy-start(bf16[1,192,2048]{2,1,0:T(8,128)(2,1)} %param.11) | copy-start | bytes 2359300
  13.3 64.4 %all-to-all-start.1 = ((bf16[1,2,192,2048]{2,1,0,3:T(2,128)(2,1)}), bf16[1,2,192,2048]{2,1,0,3:T(2,128)(2,1)S(1)}, u32[]{:S(2)}, u32[]{:S(2)}) async-start(bf16[1,2,192,2048]{2,1,0,3:T(2,128)(2,1)} %copy.60), calls=%async_computation.1 | async-start | bytes 4194304 | tf_op jit(solution)/shard_map/all_to_all | solution.py:35
  26.5 57.1 %copy-start.6 = (s32[64]{0:T(128)S(1)}, s32[64]{0:T(128)}, u32[]{:S(2)}) copy-start(s32[64]{0:T(128)} %param.9) | copy-start | bytes 772
  77.8 6.0 copy-start.2
  77.8 28.8 %all-to-all-start.4 = ((bf16[64,2,3072]{2,1,0:T(2,128)(2,1)}), bf16[64,2,3072]{2,1,0:T(2,128)(2,1)S(1)}, u32[]{:S(2)}, u32[]{:S(2)}) async-start(bf16[64,2,3072]{2,1,0:T(2,128)(2,1)} %reshape.169), calls=%async_computation.4 | async-start | bytes 1572864 | tf_op jit(solution)/shard_map/all_to_all | solution.py:36
  106.6 57.6 %all-to-all-start.2 = ((bf16[64,2,192,32]{2,3,1,0:T(8,128)(2,1)}), bf16[64,2,192,32]{2,3,1,0:T(8,128)(2,1)}, u32[]{:S(2)}, u32[]{:S(2)}) async-start(bf16[64,2,192,32]{2,3,1,0:T(8,128)(2,1)} %broadcast_select_fusion), calls=%async_computation.2 | async-start | bytes 4194304 | tf_op jit(solution)/shard_map/all_to_all | solution.py:40
  164.1 34.5 %all-to-all-start.5 = ((bf16[64,1,192,32]{2,3,1,0:T(8,128)(2,1)}), bf16[64,1,192,32]{2,3,1,0:T(8,128)(2,1)}, u32[]{:S(2)}, u32[]{:S(2)}) async-start(bf16[64,1,192,32]{2,3,1,0:T(8,128)(2,1)} %fusion.10), calls=%async_computation.5 | async-start | bytes 2097152 | tf_op jit(solution)/shard_map/all_to_all | solution.py:41
  204.5 5.6 copy-start.4
  204.5 76.8 %all-to-all-start.3 = ((bf16[1,2,768,2048]{3,1,0,2:T(2,128)(2,1)}), bf16[1,2,768,2048]{3,1,0,2:T(2,128)(2,1)}, u32[]{:S(2)}, u32[]{:S(2)}) async-start(bf16[1,2,768,2048]{3,1,0,2:T(2,128)(2,1)} %bitcast.81), calls=%async_computation.3 | async-start | bytes 12582912 | tf_op jit(solution)/shard_map/all_to_all | solution.py:9
  281.3 147.5 %all-to-all-start = ((bf16[64,24,2048]{2,1,0:T(8,128)(2,1)}), bf16[64,24,2048]{2,1,0:T(8,128)(2,1)}, u32[]{:S(2)}, u32[]{:S(2)}) async-start(bf16[64,24,2048]{2,1,0:T(8,128)(2,1)} %bitcast.80), calls=%async_computation | async-start | bytes 12582912 | tf_op jit(solution)/shard_map/all_to_all | solution.py:57
  288.0 156.4 %all-gather.2.cloned.1.call-start = ((), (), s32[]{:S(2)}) async-start(), calls=%async_computation.7 | async-start | bytes 3932160 | tf_op jit(solution)/shard_map/all_gather | solution.py:45
  455.8 6.1 copy-start.5
  455.8 146.9 %all-to-all-start.6 = ((bf16[64,24,2048]{2,1,0:T(8,128)(2,1)}), bf16[64,24,2048]{2,1,0:T(8,128)(2,1)}, u32[]{:S(2)}, u32[]{:S(2)}) async-start(bf16[64,24,2048]{2,1,0:T(8,128)(2,1)} %bitcast.88), calls=%async_computation.6 | async-start | bytes 12582912 | tf_op jit(solution)/shard_map/all_to_all | solution.py:67
  602.7 19.3 %copy-start.1 = (bf16[128,2048]{1,0:T(8,128)(2,1)S(1)}, bf16[128,2048]{1,0:T(8,128)(2,1)}, u32[]{:S(2)}) copy-start(bf16[128,2048]{1,0:T(8,128)(2,1)} %param.6) | copy-start | bytes 1572868
Sparse Core Ops, SparseCore 0:
  291.2 41.1 all-gather.1
